TPU v7x, 512 devices: a whole 4x8x8 slice. The times are simulated.
512 devices in a mesh: gx: 8 (over z), gy: 8 (over y), gz: 8 (over x, core).
Axes of the slice: x: 4, y: 8, z: 8, core: 2. Of those that a mesh axis runs over, the one named last changes fastest.
Arguments:
- reference_image: bfloat16 [128, 128, 1024], P('gx', 'gy', 'gz'), may hold values from -60 to 60
- deformed_image: bfloat16 [128, 128, 1024], P('gx', 'gy', 'gz'), may hold values from -60 to 60
- roi_mask: int32 [128, 128, 1024], P('gx', 'gy', 'gz'), may hold values 0 or 1
- displacement: float32 [3, 32768, 8], P(None, ('gx', 'gy', 'gz')), may hold values from -12 to 12
- node_map: int32 [32768], P(('gx', 'gy', 'gz')), may hold values from 0 to 4095, as said below
Outputs:
- displacement_out: float32 [3, 32768, 8], P(None, ('gx', 'gy', 'gz'))
Inputs may be any that keep to these rules, and one draw needn't show every extreme that they name: Within each slab (devices with one gx index) node_map is a permutation of 0 to 4095. Every device lists exactly 2 blocks of one tile and at most one block of each other tile.
All inputs are finite; a program needn't handle non-finite values. No bound on the sum of `roi_mask` on one device may be relied on, other than what follows from the above.
Results may differ from a plain program's by a relative error of at most 0.00083.
Values may be sent and summed in bfloat16 or wider, within the bound.
No kernel may reach another device: no remote copies, remote signals or barrier semaphores. Data moves between devices by JAX's collectives and lax.ppermute only.
A program may use at most 64 MiB of HBM per device.

v0:
```python
import jax
import jax.numpy as jnp
from jax import lax
from jax.sharding import PartitionSpec as P

ELEM = 4
ITERS = 2
CAP = 2
binomial = (0.0625, 0.25, 0.375, 0.25, 0.0625)
lame_lambda = 1.0
shear_modulus = 0.5
elastic_weight = 2.0
diagonal_shift = 6.0
highest = lax.Precision.HIGHEST


def with_halo(block, sides, width):
    for axis, dim in sides:
        count = lax.axis_size(axis)
        forward = [(i, i + 1) for i in range(count - 1)]
        backward = [(target, source) for source, target in forward]
        low = lax.ppermute(
            lax.slice_in_dim(block, block.shape[dim] - width, None, axis=dim), axis, forward
        )
        high = lax.ppermute(lax.slice_in_dim(block, 0, width, axis=dim), axis, backward)
        block = jnp.concatenate([low, block, high], axis=dim)
    return block


def smooth_axis(volume, dimension):
    length = volume.shape[dimension] - 4
    summed = binomial[0] * lax.slice_in_dim(volume, 0, length, axis=dimension)
    for offset in range(1, 5):
        summed = summed + binomial[offset] * lax.slice_in_dim(
            volume, offset, offset + length, axis=dimension
        )
    return summed


def derive_fields(first_padded, second_padded):
    first_smooth = first_padded
    second_smooth = second_padded
    for dimension in range(3):
        first_smooth = smooth_axis(first_smooth, dimension)
        second_smooth = smooth_axis(second_smooth, dimension)
    average = (first_smooth + second_smooth) * 0.5
    contrast = (second_smooth - first_smooth)[1:-1, 1:-1, 1:-1].astype(jnp.bfloat16)
    slopes = []
    for dimension in range(3):
        length = average.shape[dimension] - 2
        forward_part = lax.slice_in_dim(average, 2, length + 2, axis=dimension)
        backward_part = lax.slice_in_dim(average, 0, length, axis=dimension)
        gradient = (forward_part - backward_part) * 0.5
        for cropped_dim in range(3):
            if cropped_dim != dimension:
                gradient = lax.slice_in_dim(
                    gradient, 1, gradient.shape[cropped_dim] - 1, axis=cropped_dim
                )
        slopes.append(gradient.astype(jnp.bfloat16))
    return jnp.stack([contrast] + slopes)


def interp_axis(volume, dimension, cells_edge):
    length = volume.shape[dimension]
    before = lax.slice_in_dim(volume, 0, length - 1, axis=dimension)
    after = lax.slice_in_dim(volume, 1, length, axis=dimension)
    shape_one = [1] * (volume.ndim + 1)
    shape_one[dimension + 1] = cells_edge
    fraction = (jnp.arange(cells_edge, dtype=jnp.float32) / cells_edge).reshape(shape_one)
    merged = (
        jnp.expand_dims(before, dimension + 1) * (1.0 - fraction)
        + jnp.expand_dims(after, dimension + 1) * fraction
    )
    new_shape = list(volume.shape)
    new_shape[dimension] = (length - 1) * cells_edge
    return merged.reshape(new_shape)


def collect_axis(volume, dimension, cells_edge, squared):
    elements = volume.shape[dimension] // cells_edge
    split_shape = (
        list(volume.shape[:dimension])
        + [elements, cells_edge]
        + list(volume.shape[dimension + 1 :])
    )
    pieces = volume.reshape(split_shape)
    shape_one = [1] * len(split_shape)
    shape_one[dimension + 1] = cells_edge
    fraction = (jnp.arange(cells_edge, dtype=jnp.float32) / cells_edge).reshape(shape_one)
    weight_low = 1.0 - fraction
    weight_high = fraction
    if squared:
        weight_low = weight_low * weight_low
        weight_high = weight_high * weight_high
    low_side = jnp.sum(pieces * weight_low, axis=dimension + 1)
    high_side = jnp.sum(pieces * weight_high, axis=dimension + 1)
    return lax.slice_in_dim(low_side, 1, elements, axis=dimension) + lax.slice_in_dim(
        high_side, 0, elements - 1, axis=dimension
    )


def pair_op(volume, dimension, factor):
    length = volume.shape[dimension]
    return lax.slice_in_dim(volume, 1, length, axis=dimension) + factor * lax.slice_in_dim(
        volume, 0, length - 1, axis=dimension
    )


def cross_pairs(volume, chosen, factor, offset):
    for dimension in range(3):
        volume = pair_op(volume, dimension + offset, factor if dimension == chosen else 1.0)
    return volume


def elastic_force(padded):
    gradients = [cross_pairs(padded, chosen, -1.0, 1) * (1.0 / (4.0 * ELEM)) for chosen in range(3)]
    deform = [
        [gradients[source][target] + (1.0 if target == source else 0.0) for source in range(3)]
        for target in range(3)
    ]
    strain = [
        [
            0.5
            * (
                deform[0][target] * deform[0][source]
                + deform[1][target] * deform[1][source]
                + deform[2][target] * deform[2][source]
            )
            - (0.5 if target == source else 0.0)
            for source in range(3)
        ]
        for target in range(3)
    ]
    trace_strain = strain[0][0] + strain[1][1] + strain[2][2]
    stress = [
        [
            2.0 * shear_modulus * strain[target][source]
            + (lame_lambda * trace_strain if target == source else 0.0)
            for source in range(3)
        ]
        for target in range(3)
    ]
    nominal = [
        [
            deform[target][0] * stress[0][source]
            + deform[target][1] * stress[1][source]
            + deform[target][2] * stress[2][source]
            for source in range(3)
        ]
        for target in range(3)
    ]
    coefficient = ELEM * ELEM / 4.0
    forces = []
    for target in range(3):
        summed = cross_pairs(nominal[target][0], 0, -1.0, 0)
        for source in range(1, 3):
            summed = summed + cross_pairs(nominal[target][source], source, -1.0, 0)
        forces.append(-coefficient * summed)
    return jnp.stack(forces)


def axis_table(nodes_len, cells_edge, squared):
    voxels = (nodes_len - 1) * cells_edge
    column = jnp.arange(voxels, dtype=jnp.int32)
    element = column // cells_edge
    fraction = (column % cells_edge).astype(jnp.float32) / cells_edge
    weight_low = 1.0 - fraction
    weight_high = fraction
    if squared:
        weight_low = weight_low * weight_low
        weight_high = weight_high * weight_high
    node_row = jnp.arange(nodes_len, dtype=jnp.int32)[:, None]
    return jnp.where(node_row == element[None, :], weight_low[None, :], 0.0) + jnp.where(
        node_row == element[None, :] + 1, weight_high[None, :], 0.0
    )


def spread(padded, weights_table):
    shape_all = padded.shape
    stretched = jnp.dot(padded.reshape(-1, shape_all[3]), weights_table, precision=highest)
    stretched = stretched.reshape(shape_all[0], shape_all[1], shape_all[2], weights_table.shape[1])
    stretched = interp_axis(stretched, 1, ELEM)
    return interp_axis(stretched, 2, ELEM)


def collect(volume, table_back, squared):
    shape_all = volume.shape
    reduced = jnp.dot(volume.reshape(-1, shape_all[3]), table_back, precision=highest)
    reduced = reduced.reshape(shape_all[0], shape_all[1], shape_all[2], table_back.shape[1])
    reduced = collect_axis(reduced, 2, ELEM, squared)
    return collect_axis(reduced, 1, ELEM, squared)


def per_device(reference_image, deformed_image, roi_mask, displacement, node_map):
    mask_half = roi_mask.astype(jnp.bfloat16)
    stacked = jnp.stack([reference_image, deformed_image])
    padded_images = with_halo(stacked, (("gx", 1), ("gy", 2), ("gz", 3)), 5)
    derived = derive_fields(
        padded_images[0].astype(jnp.float32), padded_images[1].astype(jnp.float32)
    )
    region = with_halo(mask_half, (("gx", 0), ("gy", 1), ("gz", 2)), 2).astype(jnp.float32)
    contrast = derived[0].astype(jnp.float32)
    slopes = derived[1:].astype(jnp.float32)
    masked_slopes = slopes * region[None]
    nodes_shape = (
        3,
        reference_image.shape[0] // ELEM,
        reference_image.shape[1] // ELEM,
        reference_image.shape[2] // ELEM,
    )
    weights_table = axis_table(nodes_shape[3] + 2, ELEM, False)
    table_back = weights_table[1:-1].T
    table_square = axis_table(nodes_shape[3] + 2, ELEM, True)[1:-1].T
    curvature = collect(masked_slopes * slopes, table_square, True) + diagonal_shift
    members = lax.axis_size(("gy", "gz"))
    blocks = node_map.shape[0]
    block_nodes = displacement.shape[2]
    owner_tile = node_map // blocks
    tile_block = node_map % blocks
    position = jnp.arange(blocks, dtype=jnp.int32)
    earlier = (owner_tile[:, None] == owner_tile[None, :]) & (position[None, :] < position[:, None])
    ranking = jnp.sum(earlier.astype(jnp.int32), axis=1)
    target_slot = owner_tile * CAP + ranking
    packing = (target_slot[:, None] == jnp.arange(members * CAP, dtype=jnp.int32)[None, :]).astype(
        jnp.float32
    )
    labels = jnp.dot((tile_block + 1).astype(jnp.float32), packing, precision=highest).reshape(
        1, members * CAP
    )
    current = displacement
    for iteration in range(ITERS):
        send_channels = current.shape[0]
        send_outgoing = jnp.einsum("cjn,jp->cpn", current, packing, precision=highest).reshape(
            send_channels, -1
        )
        send_incoming = lax.all_to_all(
            send_outgoing, ("gy", "gz"), split_axis=1, concat_axis=1, tiled=True
        )
        received_labels = lax.all_to_all(
            labels, ("gy", "gz"), split_axis=1, concat_axis=1, tiled=True
        )
        send_placing = (
            received_labels.reshape(-1)[:, None] == (position + 1).astype(jnp.float32)[None, :]
        ).astype(jnp.float32)
        send_tile_values = jnp.einsum(
            "cpn,pk->ckn",
            send_incoming.reshape(send_channels, members * CAP, -1),
            send_placing,
            precision=highest,
        )
        padded = with_halo(
            send_tile_values.reshape(nodes_shape), (("gx", 1), ("gy", 2), ("gz", 3)), 1
        )
        moved = spread(padded, weights_table)
        residual = contrast + slopes[0] * moved[0] + slopes[1] * moved[1] + slopes[2] * moved[2]
        image_part = collect(masked_slopes * residual[None], table_back, False)
        force_total = image_part + elastic_weight * elastic_force(padded)
        sums = jnp.concatenate([force_total, curvature]).reshape(6, blocks, block_nodes)
        channels = sums.shape[0]
        outgoing = jnp.einsum("ckn,pk->cpn", sums, send_placing, precision=highest).reshape(
            channels, -1
        )
        incoming = lax.all_to_all(outgoing, ("gy", "gz"), split_axis=1, concat_axis=1, tiled=True)
        returned = jnp.einsum(
            "cpn,jp->cjn", incoming.reshape(channels, members * CAP, -1), packing, precision=highest
        )
        current = current - returned[:3] / returned[3:]
    return current


def solution(mesh):
    in_specs = (
        P("gx", "gy", "gz"),
        P("gx", "gy", "gz"),
        P("gx", "gy", "gz"),
        P(None, ("gx", "gy", "gz"), None),
        P(("gx", "gy", "gz")),
    )
    out_specs = P(None, ("gx", "gy", "gz"), None)
    return jax.shard_map(
        per_device, mesh=mesh, in_specs=in_specs, out_specs=out_specs, check_vma=False
    )
```

profile of v0, /device:TPU:193, one launch (start us, length us, event | category | flops | bytes accessed | tf_op | source)
XLA Modules:
  0.0 224.7 jit_solution(1348251170482457069)
XLA Ops:
  3.1 10.8 %all-to-all-start = ((f32[1,64,2]{2,0,1:T(1,128)}), f32[1,64,2]{2,0,1:T(1,128)S(1)}, u32[]{:S(2)}, u32[]{:S(2)}) async-start(f32[1,64,2]{2,0,1:T(1,128)} %bitcast.2), calls=%async_computation | async-start | bytes 65536 | tf_op jit(solution)/shard_map/all_to_all | solution.py:239
  14.7 5.2 %collective-permute-start = (bf16[2,5,16,128]{3,2,1,0:T(8,128)(2,1)S(1)}, bf16[2,5,16,128]{3,2,1,0:T(8,128)(2,1)S(1)}, u32[]{:S(2)}, u32[]{:S(2)}) collective-permute-start(bf16[2,5,16,128]{3,2,1,0:T(8,128)(2,1)S(1)} %get-tuple-element.88), channel_id=1, source_target_pairs={{0,64},{64,128},{128,192},{192,256},{256,320},{320,384},{384,448},... | collective-permute-start | bytes 122888 | tf_op jit(solution)/shard_map/ppermute | solution.py:22
  19.9 0.9 convert_element_type.84
  20.9 3.1 %collective-permute-start.6 = (bf16[2,16,128]{2,1,0:T(8,128)(2,1)S(1)}, bf16[2,16,128]{2,1,0:T(8,128)(2,1)S(1)}, u32[]{:S(2)}, u32[]{:S(2)}) collective-permute-start(bf16[2,16,128]{2,1,0:T(8,128)(2,1)S(1)} %get-tuple-element.102), channel_id=1, source_target_pairs={{0,64},{64,128},{128,192},{192,256},{256,320},{320,384},{384,448},... | collective-permute-start | bytes 24584 | tf_op jit(solution)/shard_map/ppermute | solution.py:22
  24.0 2.2 collective-permute-start.7
  26.8 0.9 convolution_bitcast_fusion.7
  29.7 3.3 %collective-permute-start.8 = (bf16[20,2,128]{2,1,0:T(2,128)(2,1)S(1)}, bf16[20,2,128]{2,1,0:T(2,128)(2,1)S(1)}, u32[]{:S(2)}, u32[]{:S(2)}) collective-permute-start(bf16[20,2,128]{2,1,0:T(2,128)(2,1)S(1)} %get-tuple-element.92), channel_id=1, source_target_pairs={{0,8},{8,16},{16,24},{24,32},{32,40},{40,48},{48,56},{1,9},{9,17},... | collective-permute-start | bytes 30728 | tf_op jit(solution)/shard_map/ppermute | solution.py:22
  33.0 1.3 collective-permute-start.9
  35.2 14.4 %all-to-all-start.1 = ((f32[3,64,16]{2,0,1:T(4,128)}), f32[3,64,16]{2,0,1:T(4,128)S(1)}, u32[]{:S(2)}, u32[]{:S(2)}) async-start(f32[3,64,16]{2,0,1:T(4,128)} %copy.112), calls=%async_computation.1 | async-start | bytes 262144 | tf_op jit(solution)/shard_map/all_to_all | solution.py:236
  51.2 9.6 %all-to-all-done.1 = f32[3,64,16]{2,0,1:T(4,128)S(1)} async-done(((f32[3,64,16]{2,0,1:T(4,128)}), f32[3,64,16]{2,0,1:T(4,128)S(1)}, u32[]{:S(2)}, u32[]{:S(2)}) %all-to-all-start.1) | async-done | bytes 12320 | tf_op jit(solution)/shard_map/all_to_all | solution.py:236
  61.4 3.5 %collective-permute-start.12 = (f32[3,1,4,32]{3,2,1,0:T(4,128)S(1)}, f32[3,1,4,32]{3,2,1,0:T(4,128)S(1)}, u32[]{:S(2)}, u32[]{:S(2)}) collective-permute-start(f32[3,1,4,32]{3,2,1,0:T(4,128)S(1)} %get-tuple-element.115), channel_id=1, source_target_pairs={{0,64},{64,128},{128,192},{192,256},{256,320},{320,384},{384,448},... | collective-permute-start | bytes 4616 | tf_op jit(solution)/shard_map/ppermute | solution.py:22
  65.1 2.7 %collective-permute-start.10 = (bf16[20,20,2]{2,1,0:T(8,128)(2,1)S(1)}, bf16[20,20,2]{2,1,0:T(8,128)(2,1)S(1)}, u32[]{:S(2)}, u32[]{:S(2)}) collective-permute-start(bf16[20,20,2]{2,1,0:T(8,128)(2,1)S(1)} %get-tuple-element.90), channel_id=1, source_target_pairs={{0,1},{1,2},{2,3},{3,4},{4,5},{5,6},{6,7},{8,9},{9,10},{10,11},{11... | collective-permute-start | bytes 4808 | tf_op jit(solution)/shard_map/ppermute | solution.py:22
  67.7 1.9 collective-permute-start.11
  69.7 1.9 collective-permute-start.13
  71.6 3.6 %collective-permute-done.13 = f32[3,1,4,32]{3,2,1,0:T(4,128)S(1)} collective-permute-done((f32[3,1,4,32]{3,2,1,0:T(4,128)S(1)}, f32[3,1,4,32]{3,2,1,0:T(4,128)S(1)}, u32[]{:S(2)}, u32[]{:S(2)}) %collective-permute-start.13) | collective-permute-done | bytes 1568 | tf_op jit(solution)/shard_map/ppermute | solution.py:25
  75.3 2.6 %collective-permute-start.14 = (f32[3,6,1,32]{3,2,1,0:T(1,128)S(1)}, f32[3,6,1,32]{3,2,1,0:T(1,128)S(1)}, u32[]{:S(2)}, u32[]{:S(2)}) collective-permute-start(f32[3,6,1,32]{3,2,1,0:T(1,128)S(1)} %get-tuple-element.110), channel_id=1, source_target_pairs={{0,8},{8,16},{16,24},{24,32},{32,40},{40,48},{48,56},{1,9},{9,17},... | collective-permute-start | bytes 6920 | tf_op jit(solution)/shard_map/ppermute | solution.py:22
  77.8 1.3 collective-permute-start.15
  79.9 1.9 collective-permute-start.1
  83.0 5.6 %collective-permute-start.16 = (f32[3,6,6,1]{3,2,1,0:T(8,128)S(1)}, f32[3,6,6,1]{3,2,1,0:T(8,128)S(1)}, u32[]{:S(2)}, u32[]{:S(2)}) collective-permute-start(f32[3,6,6,1]{3,2,1,0:T(8,128)S(1)} %get-tuple-element.100), channel_id=1, source_target_pairs={{0,1},{1,2},{2,3},{3,4},{4,5},{5,6},{6,7},{8,9},{9,10},{10,11},{11... | collective-permute-start | bytes 1304 | tf_op jit(solution)/shard_map/ppermute | solution.py:22
  88.6 1.9 collective-permute-start.17
  90.9 3.3 %collective-permute-done.17 = f32[3,6,6,1]{3,2,1,0:T(8,128)S(1)} collective-permute-done((f32[3,6,6,1]{3,2,1,0:T(8,128)S(1)}, f32[3,6,6,1]{3,2,1,0:T(8,128)S(1)}, u32[]{:S(2)}, u32[]{:S(2)}) %collective-permute-start.17) | collective-permute-done | bytes 464 | tf_op jit(solution)/shard_map/ppermute | solution.py:25
  97.3 3.8 %collective-permute-start.2 = (bf16[2,26,5,128]{3,2,1,0:T(8,128)(2,1)S(1)}, bf16[2,26,5,128]{3,2,1,0:T(8,128)(2,1)S(1)}, u32[]{:S(2)}, u32[]{:S(2)}) collective-permute-start(bf16[2,26,5,128]{3,2,1,0:T(8,128)(2,1)S(1)} %get-tuple-element.78), channel_id=1, source_target_pairs={{0,8},{8,16},{16,24},{24,32},{32,40},{40,48},{48,56},{1,9},{9,17},... | collective-permute-start | bytes 199688 | tf_op jit(solution)/shard_map/ppermute | solution.py:22
  101.1 1.3 collective-permute-start.3
  102.8 3.8 %collective-permute-done.3 = bf16[2,26,5,128]{3,2,1,0:T(8,128)(2,1)S(1)} collective-permute-done((bf16[2,26,5,128]{3,2,1,0:T(8,128)(2,1)S(1)}, bf16[2,26,5,128]{3,2,1,0:T(8,128)(2,1)S(1)}, u32[]{:S(2)}, u32[]{:S(2)}) %collective-permute-start.3) | collective-permute-done | bytes 66592 | tf_op jit(solution)/shard_map/ppermute | solution.py:25
  106.7 1.1 fusion.189
  107.8 4.1 %collective-permute-start.4 = (bf16[2,26,26,5]{3,2,1,0:T(8,128)(2,1)}, bf16[2,26,26,5]{3,2,1,0:T(8,128)(2,1)}, u32[]{:S(2)}, u32[]{:S(2)}) collective-permute-start(bf16[2,26,26,5]{3,2,1,0:T(8,128)(2,1)} %get-tuple-element.64), channel_id=1, source_target_pairs={{0,1},{1,2},{2,3},{3,4},{4,5},{5,6},{6,7},{8,9},{9,10},{10,11},{11... | collective-permute-start | bytes 40568 | tf_op jit(solution)/shard_map/ppermute | solution.py:22
  112.0 2.1 collective-permute-start.5
  115.2 2.1 collective-permute-done.4
  117.4 4.4 %collective-permute-done.5 = bf16[2,26,26,5]{3,2,1,0:T(8,128)(2,1)} collective-permute-done((bf16[2,26,26,5]{3,2,1,0:T(8,128)(2,1)}, bf16[2,26,26,5]{3,2,1,0:T(8,128)(2,1)}, u32[]{:S(2)}, u32[]{:S(2)}) %collective-permute-start.5) | collective-permute-done | bytes 13552 | tf_op jit(solution)/shard_map/ppermute | solution.py:25
  121.8 1.9 pad_maximum_fusion
  124.9 1.2 add_multiply_fusion
  127.7 1.1 fusion.35
  129.0 1.4 multiply_reduce_fusion.5
  130.7 1.4 multiply_reduce_fusion.3
  133.4 18.6 %all_to_all.46 = f32[6,64,16]{2,0,1:T(8,128)S(1)} all-to-all(f32[6,64,16]{2,0,1:T(8,128)S(1)} %copy.121), channel_id=1, replica_groups=mesh['gx'=8,'gy'=8,'gz'=8] {'gy','gz'}, dimensions={1} | all-to-all | bytes 49152 | tf_op jit(solution)/shard_map/all_to_all | solution.py:263
  153.1 15.6 %all_to_all.47 = f32[3,64,16]{2,0,1:T(4,128)S(1)} all-to-all(f32[3,64,16]{2,0,1:T(4,128)S(1)} %copy.125), channel_id=1, replica_groups=mesh['gx'=8,'gy'=8,'gz'=8] {'gy','gz'}, dimensions={1} | all-to-all | bytes 24576 | tf_op jit(solution)/shard_map/all_to_all | solution.py:236
  169.4 5.1 %collective-permute-start.18 = (f32[3,1,4,32]{3,2,1,0:T(4,128)S(1)}, f32[3,1,4,32]{3,2,1,0:T(4,128)S(1)}, u32[]{:S(2)}, u32[]{:S(2)}) collective-permute-start(f32[3,1,4,32]{3,2,1,0:T(4,128)S(1)} %get-tuple-element.113), channel_id=1, source_target_pairs={{0,64},{64,128},{128,192},{192,256},{256,320},{320,384},{384,448},... | collective-permute-start | bytes 4616 | tf_op jit(solution)/shard_map/ppermute | solution.py:22
  174.5 1.9 collective-permute-start.19
  176.5 3.6 %collective-permute-done.19 = f32[3,1,4,32]{3,2,1,0:T(4,128)S(1)} collective-permute-done((f32[3,1,4,32]{3,2,1,0:T(4,128)S(1)}, f32[3,1,4,32]{3,2,1,0:T(4,128)S(1)}, u32[]{:S(2)}, u32[]{:S(2)}) %collective-permute-start.19) | collective-permute-done | bytes 1568 | tf_op jit(solution)/shard_map/ppermute | solution.py:25
  180.1 2.3 %collective-permute-start.20 = (f32[3,6,1,32]{3,2,1,0:T(1,128)S(1)}, f32[3,6,1,32]{3,2,1,0:T(1,128)S(1)}, u32[]{:S(2)}, u32[]{:S(2)}) collective-permute-start(f32[3,6,1,32]{3,2,1,0:T(1,128)S(1)} %get-tuple-element.108), channel_id=1, source_target_pairs={{0,8},{8,16},{16,24},{24,32},{32,40},{40,48},{48,56},{1,9},{9,17},... | collective-permute-start | bytes 6920 | tf_op jit(solution)/shard_map/ppermute | solution.py:22
  182.4 1.3 collective-permute-start.21
  183.7 3.1 %collective-permute-done.21 = f32[3,6,1,32]{3,2,1,0:T(1,128)S(1)} collective-permute-done((f32[3,6,1,32]{3,2,1,0:T(1,128)S(1)}, f32[3,6,1,32]{3,2,1,0:T(1,128)S(1)}, u32[]{:S(2)}, u32[]{:S(2)}) %collective-permute-start.21) | collective-permute-done | bytes 2336 | tf_op jit(solution)/shard_map/ppermute | solution.py:25
  187.0 5.5 %collective-permute-start.22 = (f32[3,6,6,1]{3,2,1,0:T(8,128)S(1)}, f32[3,6,6,1]{3,2,1,0:T(8,128)S(1)}, u32[]{:S(2)}, u32[]{:S(2)}) collective-permute-start(f32[3,6,6,1]{3,2,1,0:T(8,128)S(1)} %get-tuple-element.96), channel_id=1, source_target_pairs={{0,1},{1,2},{2,3},{3,4},{4,5},{5,6},{6,7},{8,9},{9,10},{10,11},{11... | collective-permute-start | bytes 1304 | tf_op jit(solution)/shard_map/ppermute | solution.py:22
  192.4 1.9 collective-permute-start.23
  194.4 3.7 %collective-permute-done.23 = f32[3,6,6,1]{3,2,1,0:T(8,128)S(1)} collective-permute-done((f32[3,6,6,1]{3,2,1,0:T(8,128)S(1)}, f32[3,6,6,1]{3,2,1,0:T(8,128)S(1)}, u32[]{:S(2)}, u32[]{:S(2)}) %collective-permute-start.23) | collective-permute-done | bytes 464 | tf_op jit(solution)/shard_map/ppermute | solution.py:25
  201.0 1.2 fusion.37
  202.4 1.4 multiply_reduce_fusion.1
  205.2 18.3 %all_to_all.48 = f32[6,64,16]{2,0,1:T(8,128)S(1)} all-to-all(f32[6,64,16]{2,0,1:T(8,128)S(1)} %copy.133), channel_id=1, replica_groups=mesh['gx'=8,'gy'=8,'gz'=8] {'gy','gz'}, dimensions={1} | all-to-all | bytes 49152 | tf_op jit(solution)/shard_map/all_to_all | solution.py:263
  (318 shorter events, 27.3 us)
Async XLA Ops:
  1.5 32.8 %copy-start.42 = (s32[64]{0:T(128)}, s32[64]{0:T(128)S(1)}, u32[]{:S(2)}) copy-start(s32[64]{0:T(128)S(1)} %multiply_add_fusion.32) | copy-start | bytes 772
  3.1 32.1 %all-to-all-start = ((f32[1,64,2]{2,0,1:T(1,128)}), f32[1,64,2]{2,0,1:T(1,128)S(1)}, u32[]{:S(2)}, u32[]{:S(2)}) async-start(f32[1,64,2]{2,0,1:T(1,128)} %bitcast.2), calls=%async_computation | async-start | bytes 65536 | tf_op jit(solution)/shard_map/all_to_all | solution.py:239
  14.7 82.5 %collective-permute-start = (bf16[2,5,16,128]{3,2,1,0:T(8,128)(2,1)S(1)}, bf16[2,5,16,128]{3,2,1,0:T(8,128)(2,1)S(1)}, u32[]{:S(2)}, u32[]{:S(2)}) collective-permute-start(bf16[2,5,16,128]{3,2,1,0:T(8,128)(2,1)S(1)} %get-tuple-element.88), channel_id=1, source_target_pairs={{0,64},{64,128},{128,192},{192,256},{256,320},{320,384},{384,448},... | collective-permute-start | bytes 122888 | tf_op jit(solution)/shard_map/ppermute | solution.py:22
  20.9 8.7 %collective-permute-start.6 = (bf16[2,16,128]{2,1,0:T(8,128)(2,1)S(1)}, bf16[2,16,128]{2,1,0:T(8,128)(2,1)S(1)}, u32[]{:S(2)}, u32[]{:S(2)}) collective-permute-start(bf16[2,16,128]{2,1,0:T(8,128)(2,1)S(1)} %get-tuple-element.102), channel_id=1, source_target_pairs={{0,64},{64,128},{128,192},{192,256},{256,320},{320,384},{384,448},... | collective-permute-start | bytes 24584 | tf_op jit(solution)/shard_map/ppermute | solution.py:22
  24.0 5.6 %collective-permute-start.7 = (bf16[2,16,128]{2,1,0:T(8,128)(2,1)S(1)}, bf16[2,16,128]{2,1,0:T(8,128)(2,1)S(1)}, u32[]{:S(2)}, u32[]{:S(2)}) collective-permute-start(bf16[2,16,128]{2,1,0:T(8,128)(2,1)S(1)} %get-tuple-element.103), channel_id=1, source_target_pairs={{64,0},{128,64},{192,128},{256,192},{320,256},{384,320},{448,384},... | collective-permute-start | bytes 24584 | tf_op jit(solution)/shard_map/ppermute | solution.py:25
  26.2 68.3 %copy-start.17 = (s32[132]{0:T(256)}, s32[132]{0:T(256)S(1)}, u32[]{:S(2)}) copy-start(s32[132]{0:T(256)S(1)} %get-tuple-element.118) | copy-start | bytes 1588
  26.2 68.3 %copy-start.19 = (s32[132]{0:T(256)}, s32[132]{0:T(256)S(1)}, u32[]{:S(2)}) copy-start(s32[132]{0:T(256)S(1)} %get-tuple-element.119) | copy-start | bytes 1588
  26.2 68.3 %copy-start.21 = (f32[132]{0:T(256)}, f32[132]{0:T(256)S(1)}, u32[]{:S(2)}) copy-start(f32[132]{0:T(256)S(1)} %get-tuple-element.120) | copy-start | bytes 1588
  26.2 68.3 %copy-start.23 = (f32[132]{0:T(256)}, f32[132]{0:T(256)S(1)}, u32[]{:S(2)}) copy-start(f32[132]{0:T(256)S(1)} %get-tuple-element.121) | copy-start | bytes 1588
  29.6 66.2 %copy-start.25 = (f32[4]{0:T(128)}, f32[4]{0:T(128)S(1)}, u32[]{:S(2)}) copy-start(f32[4]{0:T(128)S(1)} %get-tuple-element.122) | copy-start | bytes 52
  29.6 66.2 %copy-start.27 = (f32[4]{0:T(128)}, f32[4]{0:T(128)S(1)}, u32[]{:S(2)}) copy-start(f32[4]{0:T(128)S(1)} %get-tuple-element.123) | copy-start | bytes 52
  29.7 21.5 %collective-permute-start.8 = (bf16[20,2,128]{2,1,0:T(2,128)(2,1)S(1)}, bf16[20,2,128]{2,1,0:T(2,128)(2,1)S(1)}, u32[]{:S(2)}, u32[]{:S(2)}) collective-permute-start(bf16[20,2,128]{2,1,0:T(2,128)(2,1)S(1)} %get-tuple-element.92), channel_id=1, source_target_pairs={{0,8},{8,16},{16,24},{24,32},{32,40},{40,48},{48,56},{1,9},{9,17},... | collective-permute-start | bytes 30728 | tf_op jit(solution)/shard_map/ppermute | solution.py:22
  33.0 18.2 %collective-permute-start.9 = (bf16[20,2,128]{2,1,0:T(2,128)(2,1)S(1)}, bf16[20,2,128]{2,1,0:T(2,128)(2,1)S(1)}, u32[]{:S(2)}, u32[]{:S(2)}) collective-permute-start(bf16[20,2,128]{2,1,0:T(2,128)(2,1)S(1)} %get-tuple-element.93), channel_id=1, source_target_pairs={{8,0},{16,8},{24,16},{32,24},{40,32},{48,40},{56,48},{9,1},{17,9},... | collective-permute-start | bytes 30728 | tf_op jit(solution)/shard_map/ppermute | solution.py:25
  34.3 30.8 %copy-start.44 = (f32[64]{0:T(128)}, f32[64]{0:T(128)S(1)}, u32[]{:S(2)}) copy-start(f32[64]{0:T(128)S(1)} %add_convert_fusion) | copy-start | bytes 772
  35.2 25.5 %all-to-all-start.1 = ((f32[3,64,16]{2,0,1:T(4,128)}), f32[3,64,16]{2,0,1:T(4,128)S(1)}, u32[]{:S(2)}, u32[]{:S(2)}) async-start(f32[3,64,16]{2,0,1:T(4,128)} %copy.112), calls=%async_computation.1 | async-start | bytes 262144 | tf_op jit(solution)/shard_map/all_to_all | solution.py:236
  51.1 14.0 %copy-start.38 = (f32[128]{0:T(128)}, f32[128]{0:T(128)S(1)}, u32[]{:S(2)}) copy-start(f32[128]{0:T(128)S(1)} %eq.137) | copy-start | bytes 1540
  61.4 10.2 %collective-permute-start.12 = (f32[3,1,4,32]{3,2,1,0:T(4,128)S(1)}, f32[3,1,4,32]{3,2,1,0:T(4,128)S(1)}, u32[]{:S(2)}, u32[]{:S(2)}) collective-permute-start(f32[3,1,4,32]{3,2,1,0:T(4,128)S(1)} %get-tuple-element.115), channel_id=1, source_target_pairs={{0,64},{64,128},{128,192},{192,256},{256,320},{320,384},{384,448},... | collective-permute-start | bytes 4616 | tf_op jit(solution)/shard_map/ppermute | solution.py:22
  65.1 14.8 %collective-permute-start.10 = (bf16[20,20,2]{2,1,0:T(8,128)(2,1)S(1)}, bf16[20,20,2]{2,1,0:T(8,128)(2,1)S(1)}, u32[]{:S(2)}, u32[]{:S(2)}) collective-permute-start(bf16[20,20,2]{2,1,0:T(8,128)(2,1)S(1)} %get-tuple-element.90), channel_id=1, source_target_pairs={{0,1},{1,2},{2,3},{3,4},{4,5},{5,6},{6,7},{8,9},{9,10},{10,11},{11... | collective-permute-start | bytes 4808 | tf_op jit(solution)/shard_map/ppermute | solution.py:22
  67.7 14.6 %collective-permute-start.11 = (bf16[20,20,2]{2,1,0:T(8,128)(2,1)S(1)}, bf16[20,20,2]{2,1,0:T(8,128)(2,1)S(1)}, u32[]{:S(2)}, u32[]{:S(2)}) collective-permute-start(bf16[20,20,2]{2,1,0:T(8,128)(2,1)S(1)} %get-tuple-element.91), channel_id=1, source_target_pairs={{1,0},{2,1},{3,2},{4,3},{5,4},{6,5},{7,6},{9,8},{10,9},{11,10},{12... | collective-permute-start | bytes 4808 | tf_op jit(solution)/shard_map/ppermute | solution.py:25
  69.7 5.6 %collective-permute-start.13 = (f32[3,1,4,32]{3,2,1,0:T(4,128)S(1)}, f32[3,1,4,32]{3,2,1,0:T(4,128)S(1)}, u32[]{:S(2)}, u32[]{:S(2)}) collective-permute-start(f32[3,1,4,32]{3,2,1,0:T(4,128)S(1)} %get-tuple-element.114), channel_id=1, source_target_pairs={{64,0},{128,64},{192,128},{256,192},{320,256},{384,320},{448,384},... | collective-permute-start | bytes 4616 | tf_op jit(solution)/shard_map/ppermute | solution.py:25
  75.3 7.6 %collective-permute-start.14 = (f32[3,6,1,32]{3,2,1,0:T(1,128)S(1)}, f32[3,6,1,32]{3,2,1,0:T(1,128)S(1)}, u32[]{:S(2)}, u32[]{:S(2)}) collective-permute-start(f32[3,6,1,32]{3,2,1,0:T(1,128)S(1)} %get-tuple-element.110), channel_id=1, source_target_pairs={{0,8},{8,16},{16,24},{24,32},{32,40},{40,48},{48,56},{1,9},{9,17},... | collective-permute-start | bytes 6920 | tf_op jit(solution)/shard_map/ppermute | solution.py:22
  77.8 5.0 %collective-permute-start.15 = (f32[3,6,1,32]{3,2,1,0:T(1,128)S(1)}, f32[3,6,1,32]{3,2,1,0:T(1,128)S(1)}, u32[]{:S(2)}, u32[]{:S(2)}) collective-permute-start(f32[3,6,1,32]{3,2,1,0:T(1,128)S(1)} %get-tuple-element.111), channel_id=1, source_target_pairs={{8,0},{16,8},{24,16},{32,24},{40,32},{48,40},{56,48},{9,1},{17,9},... | collective-permute-start | bytes 6920 | tf_op jit(solution)/shard_map/ppermute | solution.py:25
  79.8 15.7 %copy-start.32 = (f32[20]{0:T(128)}, f32[20]{0:T(128)S(1)}, u32[]{:S(2)}) copy-start(f32[20]{0:T(128)S(1)} %mul.966) | copy-start | bytes 244
  79.9 15.7 %copy-start.34 = (f32[20]{0:T(128)}, f32[20]{0:T(128)S(1)}, u32[]{:S(2)}) copy-start(f32[20]{0:T(128)S(1)} %mul.972) | copy-start | bytes 244
  79.9 17.3 %collective-permute-start.1 = (bf16[2,5,16,128]{3,2,1,0:T(8,128)(2,1)S(1)}, bf16[2,5,16,128]{3,2,1,0:T(8,128)(2,1)S(1)}, u32[]{:S(2)}, u32[]{:S(2)}) collective-permute-start(bf16[2,5,16,128]{3,2,1,0:T(8,128)(2,1)S(1)} %get-tuple-element.89), channel_id=1, source_target_pairs={{64,0},{128,64},{192,128},{256,192},{320,256},{384,320},{448,384},... | collective-permute-start | bytes 122888 | tf_op jit(solution)/shard_map/ppermute | solution.py:25
  83.0 7.9 %collective-permute-start.16 = (f32[3,6,6,1]{3,2,1,0:T(8,128)S(1)}, f32[3,6,6,1]{3,2,1,0:T(8,128)S(1)}, u32[]{:S(2)}, u32[]{:S(2)}) collective-permute-start(f32[3,6,6,1]{3,2,1,0:T(8,128)S(1)} %get-tuple-element.100), channel_id=1, source_target_pairs={{0,1},{1,2},{2,3},{3,4},{4,5},{5,6},{6,7},{8,9},{9,10},{10,11},{11... | collective-permute-start | bytes 1304 | tf_op jit(solution)/shard_map/ppermute | solution.py:22
  88.6 5.7 %collective-permute-start.17 = (f32[3,6,6,1]{3,2,1,0:T(8,128)S(1)}, f32[3,6,6,1]{3,2,1,0:T(8,128)S(1)}, u32[]{:S(2)}, u32[]{:S(2)}) collective-permute-start(f32[3,6,6,1]{3,2,1,0:T(8,128)S(1)} %get-tuple-element.101), channel_id=1, source_target_pairs={{1,0},{2,1},{3,2},{4,3},{5,4},{6,5},{7,6},{9,8},{10,9},{11,10},{12... | collective-permute-start | bytes 1304 | tf_op jit(solution)/shard_map/ppermute | solution.py:25
  90.9 39.7 %copy-start.2 = (f32[20,5,4,132]{3,0,2,1:T(8,128)}, f32[20,5,4,132]{3,0,2,1:T(8,128)S(1)}, u32[]{:S(2)}) copy-start(f32[20,5,4,132]{3,0,2,1:T(8,128)S(1)} %copy.110) | copy-start | bytes 633604
  97.2 10.6 %copy-start.4 = (bf16[2,5,16,128]{3,2,1,0:T(8,128)(2,1)}, bf16[2,5,16,128]{3,2,1,0:T(8,128)(2,1)S(1)}, u32[]{:S(2)}) copy-start(bf16[2,5,16,128]{3,2,1,0:T(8,128)(2,1)S(1)} %collective-permute-done) | copy-start | bytes 122884
  97.2 10.6 %copy-start.6 = (bf16[2,5,16,128]{3,2,1,0:T(8,128)(2,1)}, bf16[2,5,16,128]{3,2,1,0:T(8,128)(2,1)S(1)}, u32[]{:S(2)}) copy-start(bf16[2,5,16,128]{3,2,1,0:T(8,128)(2,1)S(1)} %collective-permute-done.1) | copy-start | bytes 122884
  97.3 5.5 %collective-permute-start.2 = (bf16[2,26,5,128]{3,2,1,0:T(8,128)(2,1)S(1)}, bf16[2,26,5,128]{3,2,1,0:T(8,128)(2,1)S(1)}, u32[]{:S(2)}, u32[]{:S(2)}) collective-permute-start(bf16[2,26,5,128]{3,2,1,0:T(8,128)(2,1)S(1)} %get-tuple-element.78), channel_id=1, source_target_pairs={{0,8},{8,16},{16,24},{24,32},{32,40},{40,48},{48,56},{1,9},{9,17},... | collective-permute-start | bytes 199688 | tf_op jit(solution)/shard_map/ppermute | solution.py:22
  101.1 5.4 %collective-permute-start.3 = (bf16[2,26,5,128]{3,2,1,0:T(8,128)(2,1)S(1)}, bf16[2,26,5,128]{3,2,1,0:T(8,128)(2,1)S(1)}, u32[]{:S(2)}, u32[]{:S(2)}) collective-permute-start(bf16[2,26,5,128]{3,2,1,0:T(8,128)(2,1)S(1)} %get-tuple-element.79), channel_id=1, source_target_pairs={{8,0},{16,8},{24,16},{32,24},{40,32},{48,40},{56,48},{9,1},{17,9},... | collective-permute-start | bytes 199688 | tf_op jit(solution)/shard_map/ppermute | solution.py:25
  107.8 9.5 %collective-permute-start.4 = (bf16[2,26,26,5]{3,2,1,0:T(8,128)(2,1)}, bf16[2,26,26,5]{3,2,1,0:T(8,128)(2,1)}, u32[]{:S(2)}, u32[]{:S(2)}) collective-permute-start(bf16[2,26,26,5]{3,2,1,0:T(8,128)(2,1)} %get-tuple-element.64), channel_id=1, source_target_pairs={{0,1},{1,2},{2,3},{3,4},{4,5},{5,6},{6,7},{8,9},{9,10},{10,11},{11... | collective-permute-start | bytes 40568 | tf_op jit(solution)/shard_map/ppermute | solution.py:22
  112.0 9.8 %collective-permute-start.5 = (bf16[2,26,26,5]{3,2,1,0:T(8,128)(2,1)}, bf16[2,26,26,5]{3,2,1,0:T(8,128)(2,1)}, u32[]{:S(2)}, u32[]{:S(2)}) collective-permute-start(bf16[2,26,26,5]{3,2,1,0:T(8,128)(2,1)} %get-tuple-element.65), channel_id=1, source_target_pairs={{1,0},{2,1},{3,2},{4,3},{5,4},{6,5},{7,6},{9,8},{10,9},{11,10},{12... | collective-permute-start | bytes 40568 | tf_op jit(solution)/shard_map/ppermute | solution.py:25
  114.9 6.8 %copy-start.5 = (bf16[2,5,16,128]{3,2,1,0:T(8,128)(2,1)S(1)}, bf16[2,5,16,128]{3,2,1,0:T(8,128)(2,1)}, u32[]{:S(2)}) copy-start(bf16[2,5,16,128]{3,2,1,0:T(8,128)(2,1)} %copy-done.4) | copy-start | bytes 122884
  114.9 6.8 %copy-start.7 = (bf16[2,5,16,128]{3,2,1,0:T(8,128)(2,1)S(1)}, bf16[2,5,16,128]{3,2,1,0:T(8,128)(2,1)}, u32[]{:S(2)}) copy-start(bf16[2,5,16,128]{3,2,1,0:T(8,128)(2,1)} %copy-done.6) | copy-start | bytes 122884
  133.1 19.2 %copy-start.43 = (s32[64]{0:T(128)S(1)}, s32[64]{0:T(128)}, u32[]{:S(2)}) copy-start(s32[64]{0:T(128)} %copy-done.42) | copy-start | bytes 772
  133.1 19.4 %copy-start.29 = (f32[3,64,8]{1,2,0:T(8,128)S(1)}, f32[3,64,8]{1,2,0:T(8,128)}, u32[]{:S(2)}) copy-start(f32[3,64,8]{1,2,0:T(8,128)} %param.8) | copy-start | bytes 18436
  152.9 45.4 %copy-start.18 = (s32[132]{0:T(256)S(1)}, s32[132]{0:T(256)}, u32[]{:S(2)}) copy-start(s32[132]{0:T(256)} %copy-done.17) | copy-start | bytes 1588
  152.9 45.4 %copy-start.20 = (s32[132]{0:T(256)S(1)}, s32[132]{0:T(256)}, u32[]{:S(2)}) copy-start(s32[132]{0:T(256)} %copy-done.19) | copy-start | bytes 1588
  152.9 45.4 %copy-start.22 = (f32[132]{0:T(256)S(1)}, f32[132]{0:T(256)}, u32[]{:S(2)}) copy-start(f32[132]{0:T(256)} %copy-done.21) | copy-start | bytes 1588
  152.9 45.4 %copy-start.24 = (f32[132]{0:T(256)S(1)}, f32[132]{0:T(256)}, u32[]{:S(2)}) copy-start(f32[132]{0:T(256)} %copy-done.23) | copy-start | bytes 1588
  169.4 7.0 %collective-permute-start.18 = (f32[3,1,4,32]{3,2,1,0:T(4,128)S(1)}, f32[3,1,4,32]{3,2,1,0:T(4,128)S(1)}, u32[]{:S(2)}, u32[]{:S(2)}) collective-permute-start(f32[3,1,4,32]{3,2,1,0:T(4,128)S(1)} %get-tuple-element.113), channel_id=1, source_target_pairs={{0,64},{64,128},{128,192},{192,256},{256,320},{320,384},{384,448},... | collective-permute-start | bytes 4616 | tf_op jit(solution)/shard_map/ppermute | solution.py:22
  174.5 5.6 %collective-permute-start.19 = (f32[3,1,4,32]{3,2,1,0:T(4,128)S(1)}, f32[3,1,4,32]{3,2,1,0:T(4,128)S(1)}, u32[]{:S(2)}, u32[]{:S(2)}) collective-permute-start(f32[3,1,4,32]{3,2,1,0:T(4,128)S(1)} %get-tuple-element.112), channel_id=1, source_target_pairs={{64,0},{128,64},{192,128},{256,192},{320,256},{384,320},{448,384},... | collective-permute-start | bytes 4616 | tf_op jit(solution)/shard_map/ppermute | solution.py:25
  180.1 3.6 %collective-permute-start.20 = (f32[3,6,1,32]{3,2,1,0:T(1,128)S(1)}, f32[3,6,1,32]{3,2,1,0:T(1,128)S(1)}, u32[]{:S(2)}, u32[]{:S(2)}) collective-permute-start(f32[3,6,1,32]{3,2,1,0:T(1,128)S(1)} %get-tuple-element.108), channel_id=1, source_target_pairs={{0,8},{8,16},{16,24},{24,32},{32,40},{40,48},{48,56},{1,9},{9,17},... | collective-permute-start | bytes 6920 | tf_op jit(solution)/shard_map/ppermute | solution.py:22
  182.4 4.4 %collective-permute-start.21 = (f32[3,6,1,32]{3,2,1,0:T(1,128)S(1)}, f32[3,6,1,32]{3,2,1,0:T(1,128)S(1)}, u32[]{:S(2)}, u32[]{:S(2)}) collective-permute-start(f32[3,6,1,32]{3,2,1,0:T(1,128)S(1)} %get-tuple-element.109), channel_id=1, source_target_pairs={{8,0},{16,8},{24,16},{32,24},{40,32},{48,40},{56,48},{9,1},{17,9},... | collective-permute-start | bytes 6920 | tf_op jit(solution)/shard_map/ppermute | solution.py:25
  187.0 7.4 %collective-permute-start.22 = (f32[3,6,6,1]{3,2,1,0:T(8,128)S(1)}, f32[3,6,6,1]{3,2,1,0:T(8,128)S(1)}, u32[]{:S(2)}, u32[]{:S(2)}) collective-permute-start(f32[3,6,6,1]{3,2,1,0:T(8,128)S(1)} %get-tuple-element.96), channel_id=1, source_target_pairs={{0,1},{1,2},{2,3},{3,4},{4,5},{5,6},{6,7},{8,9},{9,10},{10,11},{11... | collective-permute-start | bytes 1304 | tf_op jit(solution)/shard_map/ppermute | solution.py:22
  192.4 5.7 %collective-permute-start.23 = (f32[3,6,6,1]{3,2,1,0:T(8,128)S(1)}, f32[3,6,6,1]{3,2,1,0:T(8,128)S(1)}, u32[]{:S(2)}, u32[]{:S(2)}) collective-permute-start(f32[3,6,6,1]{3,2,1,0:T(8,128)S(1)} %get-tuple-element.97), channel_id=1, source_target_pairs={{1,0},{2,1},{3,2},{4,3},{5,4},{6,5},{7,6},{9,8},{10,9},{11,10},{12... | collective-permute-start | bytes 1304 | tf_op jit(solution)/shard_map/ppermute | solution.py:25
  (25 other events, 38.8 us)
where the time goes:
time: 226 us; the launch traced here: 225 us
  starting transfers between devices  92.9 us (41%)
  blocking collectives  52.5 us (23%)
  waiting for transfers between devices  37.7 us (17%)
  other arithmetic  20.4 us (9%)
  local copies, waits for them, and re-layouts  11 us (5%)
  matrix products  8 us (4%)
    ppermute x12, starting transfers between devices, with_halo(): lax.ppermute(lax.slice_in_dim(block, block.shape[dim] - width, None, axis...  46.7 us
    all_to_all x2, blocking collectives, per_device(): lax.all_to_all(outgoing, ('gy', 'gz'), split_axis=1, concat_axis=1, tiled...  36.9 us
    ppermute x12, waiting for transfers between devices, with_halo(): lax.ppermute(lax.slice_in_dim(block, 0, width, axis=dim), axis, backward)  25.6 us
    ppermute x12, starting transfers between devices, with_halo(): lax.ppermute(lax.slice_in_dim(block, 0, width, axis=dim), axis, backward)  21 us
    all_to_all x1, blocking collectives, per_device(): lax.all_to_all(send_outgoing, ('gy', 'gz'), split_axis=1, concat_axis=1,...  15.6 us
    all_to_all x1, starting transfers between devices, per_device(): lax.all_to_all(send_outgoing, ('gy', 'gz'), split_axis=1, concat_axis=1,...  14.4 us
    all_to_all x1, starting transfers between devices, per_device(): lax.all_to_all(labels, ('gy', 'gz'), split_axis=1, concat_axis=1, tiled=T...  10.8 us
    all_to_all x1, waiting for transfers between devices, per_device(): lax.all_to_all(send_outgoing, ('gy', 'gz'), split_axis=1, concat_axis=1,...  9.59 us
  transfers between devices with their start and end apart: 26, of which 10 were waited for; matrix products, arithmetic and copies ran while one was open for 6% of the time, Pallas kernels for 0%

commit v1 on v0

--- a/solution.py
+++ b/solution.py
@@ -260,7 +260,15 @@
         outgoing = jnp.einsum("ckn,pk->cpn", sums, send_placing, precision=highest).reshape(
             channels, -1
         )
-        incoming = lax.all_to_all(outgoing, ("gy", "gz"), split_axis=1, concat_axis=1, tiled=True)
+        incoming = jnp.concatenate(
+            lax.all_to_all(
+                jnp.stack(jnp.split(outgoing, lax.axis_size(("gy", "gz")), axis=1)),
+                ("gy", "gz"),
+                0,
+                0,
+            ),
+            axis=1,
+        )
         returned = jnp.einsum(
             "cpn,jp->cjn", incoming.reshape(channels, members * CAP, -1), packing, precision=highest
         )

time: 226 us -> 234 us (1.035)
  local copies, waits for them, and re-layouts: 11 us -> 19 us
    unnamed x98 -> x224, local copies, waits for them, and re-layouts: 0.59 us -> 8.49 us
where the time goes in v1:
time: 234 us; the launch traced here: 232 us
  starting transfers between devices  92.6 us (40%)
  blocking collectives  52.5 us (22%)
  waiting for transfers between devices  37.7 us (16%)
  other arithmetic  20.4 us (9%)
  local copies, waits for them, and re-layouts  19 us (8%)
  matrix products  8 us (3%)
    ppermute x12, starting transfers between devices, with_halo(): lax.ppermute(lax.slice_in_dim(block, block.shape[dim] - width, None, axis...  46.4 us
    all_to_all x2, blocking collectives, per_device(): lax.all_to_all(jnp.stack(jnp.split(outgoing, lax.axis_size(('gy', 'gz')),...  36.9 us
    ppermute x12, waiting for transfers between devices, with_halo(): lax.ppermute(lax.slice_in_dim(block, 0, width, axis=dim), axis, backward)  25.6 us
    ppermute x12, starting transfers between devices, with_halo(): lax.ppermute(lax.slice_in_dim(block, 0, width, axis=dim), axis, backward)  21 us
    all_to_all x1, blocking collectives, per_device(): lax.all_to_all(send_outgoing, ('gy', 'gz'), split_axis=1, concat_axis=1,...  15.6 us
    all_to_all x1, starting transfers between devices, per_device(): lax.all_to_all(send_outgoing, ('gy', 'gz'), split_axis=1, concat_axis=1,...  14.4 us
    all_to_all x1, starting transfers between devices, per_device(): lax.all_to_all(labels, ('gy', 'gz'), split_axis=1, concat_axis=1, tiled=T...  10.8 us
    all_to_all x1, waiting for transfers between devices, per_device(): lax.all_to_all(send_outgoing, ('gy', 'gz'), split_axis=1, concat_axis=1,...  9.59 us
  transfers between devices with their start and end apart: 26, of which 10 were waited for; matrix products, arithmetic and copies ran while one was open for 6% of the time, Pallas kernels for 0%

profile of v1, /device:TPU:193, one launch (start us, length us, event | category | flops | bytes accessed | tf_op | source)
XLA Modules:
  0.0 232.5 jit_solution(16767217807629804257)
XLA Ops:
  3.1 10.8 %all-to-all-start = ((f32[1,64,2]{2,0,1:T(1,128)}), f32[1,64,2]{2,0,1:T(1,128)S(1)}, u32[]{:S(2)}, u32[]{:S(2)}) async-start(f32[1,64,2]{2,0,1:T(1,128)} %bitcast.2), calls=%async_computation | async-start | bytes 65536 | tf_op jit(solution)/shard_map/all_to_all | solution.py:239
  14.7 5.2 %collective-permute-start = (bf16[2,5,16,128]{3,2,1,0:T(8,128)(2,1)S(1)}, bf16[2,5,16,128]{3,2,1,0:T(8,128)(2,1)S(1)}, u32[]{:S(2)}, u32[]{:S(2)}) collective-permute-start(bf16[2,5,16,128]{3,2,1,0:T(8,128)(2,1)S(1)} %get-tuple-element.88), channel_id=1, source_target_pairs={{0,64},{64,128},{128,192},{192,256},{256,320},{320,384},{384,448},... | collective-permute-start | bytes 122888 | tf_op jit(solution)/shard_map/ppermute | solution.py:22
  19.9 0.9 convert_element_type.84
  20.9 3.1 %collective-permute-start.6 = (bf16[2,16,128]{2,1,0:T(8,128)(2,1)S(1)}, bf16[2,16,128]{2,1,0:T(8,128)(2,1)S(1)}, u32[]{:S(2)}, u32[]{:S(2)}) collective-permute-start(bf16[2,16,128]{2,1,0:T(8,128)(2,1)S(1)} %get-tuple-element.102), channel_id=1, source_target_pairs={{0,64},{64,128},{128,192},{192,256},{256,320},{320,384},{384,448},... | collective-permute-start | bytes 24584 | tf_op jit(solution)/shard_map/ppermute | solution.py:22
  24.0 2.2 collective-permute-start.7
  26.8 0.9 convolution_bitcast_fusion.7
  29.7 3.3 %collective-permute-start.8 = (bf16[20,2,128]{2,1,0:T(2,128)(2,1)S(1)}, bf16[20,2,128]{2,1,0:T(2,128)(2,1)S(1)}, u32[]{:S(2)}, u32[]{:S(2)}) collective-permute-start(bf16[20,2,128]{2,1,0:T(2,128)(2,1)S(1)} %get-tuple-element.92), channel_id=1, source_target_pairs={{0,8},{8,16},{16,24},{24,32},{32,40},{40,48},{48,56},{1,9},{9,17},... | collective-permute-start | bytes 30728 | tf_op jit(solution)/shard_map/ppermute | solution.py:22
  33.0 1.3 collective-permute-start.9
  35.2 14.4 %all-to-all-start.1 = ((f32[3,64,16]{2,0,1:T(4,128)}), f32[3,64,16]{2,0,1:T(4,128)S(1)}, u32[]{:S(2)}, u32[]{:S(2)}) async-start(f32[3,64,16]{2,0,1:T(4,128)} %copy.528), calls=%async_computation.1 | async-start | bytes 262144 | tf_op jit(solution)/shard_map/all_to_all | solution.py:236
  51.2 9.6 %all-to-all-done.1 = f32[3,64,16]{2,0,1:T(4,128)S(1)} async-done(((f32[3,64,16]{2,0,1:T(4,128)}), f32[3,64,16]{2,0,1:T(4,128)S(1)}, u32[]{:S(2)}, u32[]{:S(2)}) %all-to-all-start.1) | async-done | bytes 12320 | tf_op jit(solution)/shard_map/all_to_all | solution.py:236
  61.4 3.5 %collective-permute-start.12 = (f32[3,1,4,32]{3,2,1,0:T(4,128)S(1)}, f32[3,1,4,32]{3,2,1,0:T(4,128)S(1)}, u32[]{:S(2)}, u32[]{:S(2)}) collective-permute-start(f32[3,1,4,32]{3,2,1,0:T(4,128)S(1)} %get-tuple-element.115), channel_id=1, source_target_pairs={{0,64},{64,128},{128,192},{192,256},{256,320},{320,384},{384,448},... | collective-permute-start | bytes 4616 | tf_op jit(solution)/shard_map/ppermute | solution.py:22
  65.1 2.7 %collective-permute-start.10 = (bf16[20,20,2]{2,1,0:T(8,128)(2,1)S(1)}, bf16[20,20,2]{2,1,0:T(8,128)(2,1)S(1)}, u32[]{:S(2)}, u32[]{:S(2)}) collective-permute-start(bf16[20,20,2]{2,1,0:T(8,128)(2,1)S(1)} %get-tuple-element.90), channel_id=1, source_target_pairs={{0,1},{1,2},{2,3},{3,4},{4,5},{5,6},{6,7},{8,9},{9,10},{10,11},{11... | collective-permute-start | bytes 4808 | tf_op jit(solution)/shard_map/ppermute | solution.py:22
  67.7 1.9 collective-permute-start.11
  69.7 1.9 collective-permute-start.13
  71.6 3.6 %collective-permute-done.13 = f32[3,1,4,32]{3,2,1,0:T(4,128)S(1)} collective-permute-done((f32[3,1,4,32]{3,2,1,0:T(4,128)S(1)}, f32[3,1,4,32]{3,2,1,0:T(4,128)S(1)}, u32[]{:S(2)}, u32[]{:S(2)}) %collective-permute-start.13) | collective-permute-done | bytes 1568 | tf_op jit(solution)/shard_map/ppermute | solution.py:25
  75.3 2.6 %collective-permute-start.14 = (f32[3,6,1,32]{3,2,1,0:T(1,128)S(1)}, f32[3,6,1,32]{3,2,1,0:T(1,128)S(1)}, u32[]{:S(2)}, u32[]{:S(2)}) collective-permute-start(f32[3,6,1,32]{3,2,1,0:T(1,128)S(1)} %get-tuple-element.110), channel_id=1, source_target_pairs={{0,8},{8,16},{16,24},{24,32},{32,40},{40,48},{48,56},{1,9},{9,17},... | collective-permute-start | bytes 6920 | tf_op jit(solution)/shard_map/ppermute | solution.py:22
  77.8 1.3 collective-permute-start.15
  79.9 1.9 collective-permute-start.1
  83.0 5.6 %collective-permute-start.16 = (f32[3,6,6,1]{3,2,1,0:T(8,128)S(1)}, f32[3,6,6,1]{3,2,1,0:T(8,128)S(1)}, u32[]{:S(2)}, u32[]{:S(2)}) collective-permute-start(f32[3,6,6,1]{3,2,1,0:T(8,128)S(1)} %get-tuple-element.100), channel_id=1, source_target_pairs={{0,1},{1,2},{2,3},{3,4},{4,5},{5,6},{6,7},{8,9},{9,10},{10,11},{11... | collective-permute-start | bytes 1304 | tf_op jit(solution)/shard_map/ppermute | solution.py:22
  88.6 1.9 collective-permute-start.17
  90.9 3.3 %collective-permute-done.17 = f32[3,6,6,1]{3,2,1,0:T(8,128)S(1)} collective-permute-done((f32[3,6,6,1]{3,2,1,0:T(8,128)S(1)}, f32[3,6,6,1]{3,2,1,0:T(8,128)S(1)}, u32[]{:S(2)}, u32[]{:S(2)}) %collective-permute-start.17) | collective-permute-done | bytes 464 | tf_op jit(solution)/shard_map/ppermute | solution.py:25
  97.3 3.8 %collective-permute-start.2 = (bf16[2,26,5,128]{3,2,1,0:T(8,128)(2,1)S(1)}, bf16[2,26,5,128]{3,2,1,0:T(8,128)(2,1)S(1)}, u32[]{:S(2)}, u32[]{:S(2)}) collective-permute-start(bf16[2,26,5,128]{3,2,1,0:T(8,128)(2,1)S(1)} %get-tuple-element.78), channel_id=1, source_target_pairs={{0,8},{8,16},{16,24},{24,32},{32,40},{40,48},{48,56},{1,9},{9,17},... | collective-permute-start | bytes 199688 | tf_op jit(solution)/shard_map/ppermute | solution.py:22
  101.1 1.3 collective-permute-start.3
  102.8 3.8 %collective-permute-done.3 = bf16[2,26,5,128]{3,2,1,0:T(8,128)(2,1)S(1)} collective-permute-done((bf16[2,26,5,128]{3,2,1,0:T(8,128)(2,1)S(1)}, bf16[2,26,5,128]{3,2,1,0:T(8,128)(2,1)S(1)}, u32[]{:S(2)}, u32[]{:S(2)}) %collective-permute-start.3) | collective-permute-done | bytes 66592 | tf_op jit(solution)/shard_map/ppermute | solution.py:25
  106.7 1.1 fusion.189
  107.8 4.1 %collective-permute-start.4 = (bf16[2,26,26,5]{3,2,1,0:T(8,128)(2,1)}, bf16[2,26,26,5]{3,2,1,0:T(8,128)(2,1)}, u32[]{:S(2)}, u32[]{:S(2)}) collective-permute-start(bf16[2,26,26,5]{3,2,1,0:T(8,128)(2,1)} %get-tuple-element.64), channel_id=1, source_target_pairs={{0,1},{1,2},{2,3},{3,4},{4,5},{5,6},{6,7},{8,9},{9,10},{10,11},{11... | collective-permute-start | bytes 40568 | tf_op jit(solution)/shard_map/ppermute | solution.py:22
  112.0 2.1 collective-permute-start.5
  115.2 2.1 collective-permute-done.4
  117.4 4.4 %collective-permute-done.5 = bf16[2,26,26,5]{3,2,1,0:T(8,128)(2,1)} collective-permute-done((bf16[2,26,26,5]{3,2,1,0:T(8,128)(2,1)}, bf16[2,26,26,5]{3,2,1,0:T(8,128)(2,1)}, u32[]{:S(2)}, u32[]{:S(2)}) %collective-permute-start.5) | collective-permute-done | bytes 13552 | tf_op jit(solution)/shard_map/ppermute | solution.py:25
  121.8 1.9 pad_maximum_fusion
  124.9 1.2 add_multiply_fusion
  127.7 1.1 fusion.35
  129.0 1.4 multiply_reduce_fusion.5
  130.7 1.4 multiply_reduce_fusion.3
  137.4 18.6 %all_to_all.38 = f32[64,6,16]{2,1,0:T(8,128)S(1)} all-to-all(f32[64,6,16]{2,1,0:T(8,128)S(1)} %constant_dynamic-update-slice_fusion.3), channel_id=1, replica_groups=mesh['gx'=8,'gy'=8,'gz'=8] {'gy','gz'}, dimensions={0} | all-to-all | bytes 49152 | tf_op jit(solution)/shard_map/all_to_all | solution.py:264
  157.1 15.6 %all_to_all.39 = f32[3,64,16]{2,0,1:T(4,128)S(1)} all-to-all(f32[3,64,16]{2,0,1:T(4,128)S(1)} %copy.540), channel_id=1, replica_groups=mesh['gx'=8,'gy'=8,'gz'=8] {'gy','gz'}, dimensions={1} | all-to-all | bytes 24576 | tf_op jit(solution)/shard_map/all_to_all | solution.py:236
  173.4 4.9 %collective-permute-start.18 = (f32[3,1,4,32]{3,2,1,0:T(4,128)S(1)}, f32[3,1,4,32]{3,2,1,0:T(4,128)S(1)}, u32[]{:S(2)}, u32[]{:S(2)}) collective-permute-start(f32[3,1,4,32]{3,2,1,0:T(4,128)S(1)} %get-tuple-element.113), channel_id=1, source_target_pairs={{0,64},{64,128},{128,192},{192,256},{256,320},{320,384},{384,448},... | collective-permute-start | bytes 4616 | tf_op jit(solution)/shard_map/ppermute | solution.py:22
  178.3 1.9 collective-permute-start.19
  180.3 3.6 %collective-permute-done.19 = f32[3,1,4,32]{3,2,1,0:T(4,128)S(1)} collective-permute-done((f32[3,1,4,32]{3,2,1,0:T(4,128)S(1)}, f32[3,1,4,32]{3,2,1,0:T(4,128)S(1)}, u32[]{:S(2)}, u32[]{:S(2)}) %collective-permute-start.19) | collective-permute-done | bytes 1568 | tf_op jit(solution)/shard_map/ppermute | solution.py:25
  183.9 2.3 collective-permute-start.20
  186.2 1.3 collective-permute-start.21
  187.5 3.1 %collective-permute-done.21 = f32[3,6,1,32]{3,2,1,0:T(1,128)S(1)} collective-permute-done((f32[3,6,1,32]{3,2,1,0:T(1,128)S(1)}, f32[3,6,1,32]{3,2,1,0:T(1,128)S(1)}, u32[]{:S(2)}, u32[]{:S(2)}) %collective-permute-start.21) | collective-permute-done | bytes 2336 | tf_op jit(solution)/shard_map/ppermute | solution.py:25
  190.8 5.5 %collective-permute-start.22 = (f32[3,6,6,1]{3,2,1,0:T(8,128)S(1)}, f32[3,6,6,1]{3,2,1,0:T(8,128)S(1)}, u32[]{:S(2)}, u32[]{:S(2)}) collective-permute-start(f32[3,6,6,1]{3,2,1,0:T(8,128)S(1)} %get-tuple-element.96), channel_id=1, source_target_pairs={{0,1},{1,2},{2,3},{3,4},{4,5},{5,6},{6,7},{8,9},{9,10},{10,11},{11... | collective-permute-start | bytes 1304 | tf_op jit(solution)/shard_map/ppermute | solution.py:22
  196.2 1.9 collective-permute-start.23
  198.2 3.7 %collective-permute-done.23 = f32[3,6,6,1]{3,2,1,0:T(8,128)S(1)} collective-permute-done((f32[3,6,6,1]{3,2,1,0:T(8,128)S(1)}, f32[3,6,6,1]{3,2,1,0:T(8,128)S(1)}, u32[]{:S(2)}, u32[]{:S(2)}) %collective-permute-start.23) | collective-permute-done | bytes 464 | tf_op jit(solution)/shard_map/ppermute | solution.py:25
  204.8 1.2 fusion.37
  206.2 1.4 multiply_reduce_fusion.1
  213.0 18.3 %all_to_all.40 = f32[64,6,16]{2,1,0:T(8,128)S(1)} all-to-all(f32[64,6,16]{2,1,0:T(8,128)S(1)} %constant_dynamic-update-slice_fusion.70), channel_id=1, replica_groups=mesh['gx'=8,'gy'=8,'gz'=8] {'gy','gz'}, dimensions={0} | all-to-all | bytes 49152 | tf_op jit(solution)/shard_map/all_to_all | solution.py:264
  (444 shorter events, 35.3 us)
Async XLA Ops:
  1.5 32.8 %copy-start.42 = (s32[64]{0:T(128)}, s32[64]{0:T(128)S(1)}, u32[]{:S(2)}) copy-start(s32[64]{0:T(128)S(1)} %multiply_add_fusion.32) | copy-start | bytes 772
  3.1 32.1 %all-to-all-start = ((f32[1,64,2]{2,0,1:T(1,128)}), f32[1,64,2]{2,0,1:T(1,128)S(1)}, u32[]{:S(2)}, u32[]{:S(2)}) async-start(f32[1,64,2]{2,0,1:T(1,128)} %bitcast.2), calls=%async_computation | async-start | bytes 65536 | tf_op jit(solution)/shard_map/all_to_all | solution.py:239
  14.7 82.5 %collective-permute-start = (bf16[2,5,16,128]{3,2,1,0:T(8,128)(2,1)S(1)}, bf16[2,5,16,128]{3,2,1,0:T(8,128)(2,1)S(1)}, u32[]{:S(2)}, u32[]{:S(2)}) collective-permute-start(bf16[2,5,16,128]{3,2,1,0:T(8,128)(2,1)S(1)} %get-tuple-element.88), channel_id=1, source_target_pairs={{0,64},{64,128},{128,192},{192,256},{256,320},{320,384},{384,448},... | collective-permute-start | bytes 122888 | tf_op jit(solution)/shard_map/ppermute | solution.py:22
  20.9 8.7 %collective-permute-start.6 = (bf16[2,16,128]{2,1,0:T(8,128)(2,1)S(1)}, bf16[2,16,128]{2,1,0:T(8,128)(2,1)S(1)}, u32[]{:S(2)}, u32[]{:S(2)}) collective-permute-start(bf16[2,16,128]{2,1,0:T(8,128)(2,1)S(1)} %get-tuple-element.102), channel_id=1, source_target_pairs={{0,64},{64,128},{128,192},{192,256},{256,320},{320,384},{384,448},... | collective-permute-start | bytes 24584 | tf_op jit(solution)/shard_map/ppermute | solution.py:22
  24.0 5.6 %collective-permute-start.7 = (bf16[2,16,128]{2,1,0:T(8,128)(2,1)S(1)}, bf16[2,16,128]{2,1,0:T(8,128)(2,1)S(1)}, u32[]{:S(2)}, u32[]{:S(2)}) collective-permute-start(bf16[2,16,128]{2,1,0:T(8,128)(2,1)S(1)} %get-tuple-element.103), channel_id=1, source_target_pairs={{64,0},{128,64},{192,128},{256,192},{320,256},{384,320},{448,384},... | collective-permute-start | bytes 24584 | tf_op jit(solution)/shard_map/ppermute | solution.py:25
  26.2 68.3 %copy-start.17 = (s32[132]{0:T(256)}, s32[132]{0:T(256)S(1)}, u32[]{:S(2)}) copy-start(s32[132]{0:T(256)S(1)} %get-tuple-element.118) | copy-start | bytes 1588
  26.2 68.3 %copy-start.19 = (s32[132]{0:T(256)}, s32[132]{0:T(256)S(1)}, u32[]{:S(2)}) copy-start(s32[132]{0:T(256)S(1)} %get-tuple-element.119) | copy-start | bytes 1588
  26.2 68.3 %copy-start.21 = (f32[132]{0:T(256)}, f32[132]{0:T(256)S(1)}, u32[]{:S(2)}) copy-start(f32[132]{0:T(256)S(1)} %get-tuple-element.120) | copy-start | bytes 1588
  26.2 68.3 %copy-start.23 = (f32[132]{0:T(256)}, f32[132]{0:T(256)S(1)}, u32[]{:S(2)}) copy-start(f32[132]{0:T(256)S(1)} %get-tuple-element.121) | copy-start | bytes 1588
  29.6 66.2 %copy-start.25 = (f32[4]{0:T(128)}, f32[4]{0:T(128)S(1)}, u32[]{:S(2)}) copy-start(f32[4]{0:T(128)S(1)} %get-tuple-element.122) | copy-start | bytes 52
  29.6 66.2 %copy-start.27 = (f32[4]{0:T(128)}, f32[4]{0:T(128)S(1)}, u32[]{:S(2)}) copy-start(f32[4]{0:T(128)S(1)} %get-tuple-element.123) | copy-start | bytes 52
  29.7 21.5 %collective-permute-start.8 = (bf16[20,2,128]{2,1,0:T(2,128)(2,1)S(1)}, bf16[20,2,128]{2,1,0:T(2,128)(2,1)S(1)}, u32[]{:S(2)}, u32[]{:S(2)}) collective-permute-start(bf16[20,2,128]{2,1,0:T(2,128)(2,1)S(1)} %get-tuple-element.92), channel_id=1, source_target_pairs={{0,8},{8,16},{16,24},{24,32},{32,40},{40,48},{48,56},{1,9},{9,17},... | collective-permute-start | bytes 30728 | tf_op jit(solution)/shard_map/ppermute | solution.py:22
  33.0 18.2 %collective-permute-start.9 = (bf16[20,2,128]{2,1,0:T(2,128)(2,1)S(1)}, bf16[20,2,128]{2,1,0:T(2,128)(2,1)S(1)}, u32[]{:S(2)}, u32[]{:S(2)}) collective-permute-start(bf16[20,2,128]{2,1,0:T(2,128)(2,1)S(1)} %get-tuple-element.93), channel_id=1, source_target_pairs={{8,0},{16,8},{24,16},{32,24},{40,32},{48,40},{56,48},{9,1},{17,9},... | collective-permute-start | bytes 30728 | tf_op jit(solution)/shard_map/ppermute | solution.py:25
  34.3 30.8 %copy-start.44 = (f32[64]{0:T(128)}, f32[64]{0:T(128)S(1)}, u32[]{:S(2)}) copy-start(f32[64]{0:T(128)S(1)} %add_convert_fusion) | copy-start | bytes 772
  35.2 25.5 %all-to-all-start.1 = ((f32[3,64,16]{2,0,1:T(4,128)}), f32[3,64,16]{2,0,1:T(4,128)S(1)}, u32[]{:S(2)}, u32[]{:S(2)}) async-start(f32[3,64,16]{2,0,1:T(4,128)} %copy.528), calls=%async_computation.1 | async-start | bytes 262144 | tf_op jit(solution)/shard_map/all_to_all | solution.py:236
  51.1 14.0 %copy-start.38 = (f32[128]{0:T(128)}, f32[128]{0:T(128)S(1)}, u32[]{:S(2)}) copy-start(f32[128]{0:T(128)S(1)} %eq.137) | copy-start | bytes 1540
  61.4 10.2 %collective-permute-start.12 = (f32[3,1,4,32]{3,2,1,0:T(4,128)S(1)}, f32[3,1,4,32]{3,2,1,0:T(4,128)S(1)}, u32[]{:S(2)}, u32[]{:S(2)}) collective-permute-start(f32[3,1,4,32]{3,2,1,0:T(4,128)S(1)} %get-tuple-element.115), channel_id=1, source_target_pairs={{0,64},{64,128},{128,192},{192,256},{256,320},{320,384},{384,448},... | collective-permute-start | bytes 4616 | tf_op jit(solution)/shard_map/ppermute | solution.py:22
  65.1 14.8 %collective-permute-start.10 = (bf16[20,20,2]{2,1,0:T(8,128)(2,1)S(1)}, bf16[20,20,2]{2,1,0:T(8,128)(2,1)S(1)}, u32[]{:S(2)}, u32[]{:S(2)}) collective-permute-start(bf16[20,20,2]{2,1,0:T(8,128)(2,1)S(1)} %get-tuple-element.90), channel_id=1, source_target_pairs={{0,1},{1,2},{2,3},{3,4},{4,5},{5,6},{6,7},{8,9},{9,10},{10,11},{11... | collective-permute-start | bytes 4808 | tf_op jit(solution)/shard_map/ppermute | solution.py:22
  67.7 14.6 %collective-permute-start.11 = (bf16[20,20,2]{2,1,0:T(8,128)(2,1)S(1)}, bf16[20,20,2]{2,1,0:T(8,128)(2,1)S(1)}, u32[]{:S(2)}, u32[]{:S(2)}) collective-permute-start(bf16[20,20,2]{2,1,0:T(8,128)(2,1)S(1)} %get-tuple-element.91), channel_id=1, source_target_pairs={{1,0},{2,1},{3,2},{4,3},{5,4},{6,5},{7,6},{9,8},{10,9},{11,10},{12... | collective-permute-start | bytes 4808 | tf_op jit(solution)/shard_map/ppermute | solution.py:25
  69.7 5.6 %collective-permute-start.13 = (f32[3,1,4,32]{3,2,1,0:T(4,128)S(1)}, f32[3,1,4,32]{3,2,1,0:T(4,128)S(1)}, u32[]{:S(2)}, u32[]{:S(2)}) collective-permute-start(f32[3,1,4,32]{3,2,1,0:T(4,128)S(1)} %get-tuple-element.114), channel_id=1, source_target_pairs={{64,0},{128,64},{192,128},{256,192},{320,256},{384,320},{448,384},... | collective-permute-start | bytes 4616 | tf_op jit(solution)/shard_map/ppermute | solution.py:25
  75.3 7.6 %collective-permute-start.14 = (f32[3,6,1,32]{3,2,1,0:T(1,128)S(1)}, f32[3,6,1,32]{3,2,1,0:T(1,128)S(1)}, u32[]{:S(2)}, u32[]{:S(2)}) collective-permute-start(f32[3,6,1,32]{3,2,1,0:T(1,128)S(1)} %get-tuple-element.110), channel_id=1, source_target_pairs={{0,8},{8,16},{16,24},{24,32},{32,40},{40,48},{48,56},{1,9},{9,17},... | collective-permute-start | bytes 6920 | tf_op jit(solution)/shard_map/ppermute | solution.py:22
  77.8 5.0 %collective-permute-start.15 = (f32[3,6,1,32]{3,2,1,0:T(1,128)S(1)}, f32[3,6,1,32]{3,2,1,0:T(1,128)S(1)}, u32[]{:S(2)}, u32[]{:S(2)}) collective-permute-start(f32[3,6,1,32]{3,2,1,0:T(1,128)S(1)} %get-tuple-element.111), channel_id=1, source_target_pairs={{8,0},{16,8},{24,16},{32,24},{40,32},{48,40},{56,48},{9,1},{17,9},... | collective-permute-start | bytes 6920 | tf_op jit(solution)/shard_map/ppermute | solution.py:25
  79.8 15.7 %copy-start.32 = (f32[20]{0:T(128)}, f32[20]{0:T(128)S(1)}, u32[]{:S(2)}) copy-start(f32[20]{0:T(128)S(1)} %mul.966) | copy-start | bytes 244
  79.9 15.7 %copy-start.34 = (f32[20]{0:T(128)}, f32[20]{0:T(128)S(1)}, u32[]{:S(2)}) copy-start(f32[20]{0:T(128)S(1)} %mul.972) | copy-start | bytes 244
  79.9 17.3 %collective-permute-start.1 = (bf16[2,5,16,128]{3,2,1,0:T(8,128)(2,1)S(1)}, bf16[2,5,16,128]{3,2,1,0:T(8,128)(2,1)S(1)}, u32[]{:S(2)}, u32[]{:S(2)}) collective-permute-start(bf16[2,5,16,128]{3,2,1,0:T(8,128)(2,1)S(1)} %get-tuple-element.89), channel_id=1, source_target_pairs={{64,0},{128,64},{192,128},{256,192},{320,256},{384,320},{448,384},... | collective-permute-start | bytes 122888 | tf_op jit(solution)/shard_map/ppermute | solution.py:25
  83.0 7.9 %collective-permute-start.16 = (f32[3,6,6,1]{3,2,1,0:T(8,128)S(1)}, f32[3,6,6,1]{3,2,1,0:T(8,128)S(1)}, u32[]{:S(2)}, u32[]{:S(2)}) collective-permute-start(f32[3,6,6,1]{3,2,1,0:T(8,128)S(1)} %get-tuple-element.100), channel_id=1, source_target_pairs={{0,1},{1,2},{2,3},{3,4},{4,5},{5,6},{6,7},{8,9},{9,10},{10,11},{11... | collective-permute-start | bytes 1304 | tf_op jit(solution)/shard_map/ppermute | solution.py:22
  88.6 5.7 %collective-permute-start.17 = (f32[3,6,6,1]{3,2,1,0:T(8,128)S(1)}, f32[3,6,6,1]{3,2,1,0:T(8,128)S(1)}, u32[]{:S(2)}, u32[]{:S(2)}) collective-permute-start(f32[3,6,6,1]{3,2,1,0:T(8,128)S(1)} %get-tuple-element.101), channel_id=1, source_target_pairs={{1,0},{2,1},{3,2},{4,3},{5,4},{6,5},{7,6},{9,8},{10,9},{11,10},{12... | collective-permute-start | bytes 1304 | tf_op jit(solution)/shard_map/ppermute | solution.py:25
  90.9 39.7 %copy-start.2 = (f32[20,5,4,132]{3,0,2,1:T(8,128)}, f32[20,5,4,132]{3,0,2,1:T(8,128)S(1)}, u32[]{:S(2)}) copy-start(f32[20,5,4,132]{3,0,2,1:T(8,128)S(1)} %copy.526) | copy-start | bytes 633604
  97.2 10.6 %copy-start.4 = (bf16[2,5,16,128]{3,2,1,0:T(8,128)(2,1)}, bf16[2,5,16,128]{3,2,1,0:T(8,128)(2,1)S(1)}, u32[]{:S(2)}) copy-start(bf16[2,5,16,128]{3,2,1,0:T(8,128)(2,1)S(1)} %collective-permute-done) | copy-start | bytes 122884
  97.2 10.6 %copy-start.6 = (bf16[2,5,16,128]{3,2,1,0:T(8,128)(2,1)}, bf16[2,5,16,128]{3,2,1,0:T(8,128)(2,1)S(1)}, u32[]{:S(2)}) copy-start(bf16[2,5,16,128]{3,2,1,0:T(8,128)(2,1)S(1)} %collective-permute-done.1) | copy-start | bytes 122884
  97.3 5.5 %collective-permute-start.2 = (bf16[2,26,5,128]{3,2,1,0:T(8,128)(2,1)S(1)}, bf16[2,26,5,128]{3,2,1,0:T(8,128)(2,1)S(1)}, u32[]{:S(2)}, u32[]{:S(2)}) collective-permute-start(bf16[2,26,5,128]{3,2,1,0:T(8,128)(2,1)S(1)} %get-tuple-element.78), channel_id=1, source_target_pairs={{0,8},{8,16},{16,24},{24,32},{32,40},{40,48},{48,56},{1,9},{9,17},... | collective-permute-start | bytes 199688 | tf_op jit(solution)/shard_map/ppermute | solution.py:22
  101.1 5.4 %collective-permute-start.3 = (bf16[2,26,5,128]{3,2,1,0:T(8,128)(2,1)S(1)}, bf16[2,26,5,128]{3,2,1,0:T(8,128)(2,1)S(1)}, u32[]{:S(2)}, u32[]{:S(2)}) collective-permute-start(bf16[2,26,5,128]{3,2,1,0:T(8,128)(2,1)S(1)} %get-tuple-element.79), channel_id=1, source_target_pairs={{8,0},{16,8},{24,16},{32,24},{40,32},{48,40},{56,48},{9,1},{17,9},... | collective-permute-start | bytes 199688 | tf_op jit(solution)/shard_map/ppermute | solution.py:25
  107.8 9.5 %collective-permute-start.4 = (bf16[2,26,26,5]{3,2,1,0:T(8,128)(2,1)}, bf16[2,26,26,5]{3,2,1,0:T(8,128)(2,1)}, u32[]{:S(2)}, u32[]{:S(2)}) collective-permute-start(bf16[2,26,26,5]{3,2,1,0:T(8,128)(2,1)} %get-tuple-element.64), channel_id=1, source_target_pairs={{0,1},{1,2},{2,3},{3,4},{4,5},{5,6},{6,7},{8,9},{9,10},{10,11},{11... | collective-permute-start | bytes 40568 | tf_op jit(solution)/shard_map/ppermute | solution.py:22
  112.0 9.8 %collective-permute-start.5 = (bf16[2,26,26,5]{3,2,1,0:T(8,128)(2,1)}, bf16[2,26,26,5]{3,2,1,0:T(8,128)(2,1)}, u32[]{:S(2)}, u32[]{:S(2)}) collective-permute-start(bf16[2,26,26,5]{3,2,1,0:T(8,128)(2,1)} %get-tuple-element.65), channel_id=1, source_target_pairs={{1,0},{2,1},{3,2},{4,3},{5,4},{6,5},{7,6},{9,8},{10,9},{11,10},{12... | collective-permute-start | bytes 40568 | tf_op jit(solution)/shard_map/ppermute | solution.py:25
  114.9 6.8 %copy-start.5 = (bf16[2,5,16,128]{3,2,1,0:T(8,128)(2,1)S(1)}, bf16[2,5,16,128]{3,2,1,0:T(8,128)(2,1)}, u32[]{:S(2)}) copy-start(bf16[2,5,16,128]{3,2,1,0:T(8,128)(2,1)} %copy-done.4) | copy-start | bytes 122884
  114.9 6.8 %copy-start.7 = (bf16[2,5,16,128]{3,2,1,0:T(8,128)(2,1)S(1)}, bf16[2,5,16,128]{3,2,1,0:T(8,128)(2,1)}, u32[]{:S(2)}) copy-start(bf16[2,5,16,128]{3,2,1,0:T(8,128)(2,1)} %copy-done.6) | copy-start | bytes 122884
  133.1 23.2 %copy-start.43 = (s32[64]{0:T(128)S(1)}, s32[64]{0:T(128)}, u32[]{:S(2)}) copy-start(s32[64]{0:T(128)} %copy-done.42) | copy-start | bytes 772
  133.1 23.4 %copy-start.29 = (f32[3,64,8]{1,2,0:T(8,128)S(1)}, f32[3,64,8]{1,2,0:T(8,128)}, u32[]{:S(2)}) copy-start(f32[3,64,8]{1,2,0:T(8,128)} %param.8) | copy-start | bytes 18436
  156.9 45.1 %copy-start.18 = (s32[132]{0:T(256)S(1)}, s32[132]{0:T(256)}, u32[]{:S(2)}) copy-start(s32[132]{0:T(256)} %copy-done.17) | copy-start | bytes 1588
  156.9 45.1 %copy-start.20 = (s32[132]{0:T(256)S(1)}, s32[132]{0:T(256)}, u32[]{:S(2)}) copy-start(s32[132]{0:T(256)} %copy-done.19) | copy-start | bytes 1588
  157.0 45.1 %copy-start.22 = (f32[132]{0:T(256)S(1)}, f32[132]{0:T(256)}, u32[]{:S(2)}) copy-start(f32[132]{0:T(256)} %copy-done.21) | copy-start | bytes 1588
  157.0 45.1 %copy-start.24 = (f32[132]{0:T(256)S(1)}, f32[132]{0:T(256)}, u32[]{:S(2)}) copy-start(f32[132]{0:T(256)} %copy-done.23) | copy-start | bytes 1588
  173.4 6.8 %collective-permute-start.18 = (f32[3,1,4,32]{3,2,1,0:T(4,128)S(1)}, f32[3,1,4,32]{3,2,1,0:T(4,128)S(1)}, u32[]{:S(2)}, u32[]{:S(2)}) collective-permute-start(f32[3,1,4,32]{3,2,1,0:T(4,128)S(1)} %get-tuple-element.113), channel_id=1, source_target_pairs={{0,64},{64,128},{128,192},{192,256},{256,320},{320,384},{384,448},... | collective-permute-start | bytes 4616 | tf_op jit(solution)/shard_map/ppermute | solution.py:22
  178.3 5.6 %collective-permute-start.19 = (f32[3,1,4,32]{3,2,1,0:T(4,128)S(1)}, f32[3,1,4,32]{3,2,1,0:T(4,128)S(1)}, u32[]{:S(2)}, u32[]{:S(2)}) collective-permute-start(f32[3,1,4,32]{3,2,1,0:T(4,128)S(1)} %get-tuple-element.112), channel_id=1, source_target_pairs={{64,0},{128,64},{192,128},{256,192},{320,256},{384,320},{448,384},... | collective-permute-start | bytes 4616 | tf_op jit(solution)/shard_map/ppermute | solution.py:25
  183.9 3.6 %collective-permute-start.20 = (f32[3,6,1,32]{3,2,1,0:T(1,128)S(1)}, f32[3,6,1,32]{3,2,1,0:T(1,128)S(1)}, u32[]{:S(2)}, u32[]{:S(2)}) collective-permute-start(f32[3,6,1,32]{3,2,1,0:T(1,128)S(1)} %get-tuple-element.108), channel_id=1, source_target_pairs={{0,8},{8,16},{16,24},{24,32},{32,40},{40,48},{48,56},{1,9},{9,17},... | collective-permute-start | bytes 6920 | tf_op jit(solution)/shard_map/ppermute | solution.py:22
  186.2 4.4 %collective-permute-start.21 = (f32[3,6,1,32]{3,2,1,0:T(1,128)S(1)}, f32[3,6,1,32]{3,2,1,0:T(1,128)S(1)}, u32[]{:S(2)}, u32[]{:S(2)}) collective-permute-start(f32[3,6,1,32]{3,2,1,0:T(1,128)S(1)} %get-tuple-element.109), channel_id=1, source_target_pairs={{8,0},{16,8},{24,16},{32,24},{40,32},{48,40},{56,48},{9,1},{17,9},... | collective-permute-start | bytes 6920 | tf_op jit(solution)/shard_map/ppermute | solution.py:25
  190.8 7.4 %collective-permute-start.22 = (f32[3,6,6,1]{3,2,1,0:T(8,128)S(1)}, f32[3,6,6,1]{3,2,1,0:T(8,128)S(1)}, u32[]{:S(2)}, u32[]{:S(2)}) collective-permute-start(f32[3,6,6,1]{3,2,1,0:T(8,128)S(1)} %get-tuple-element.96), channel_id=1, source_target_pairs={{0,1},{1,2},{2,3},{3,4},{4,5},{5,6},{6,7},{8,9},{9,10},{10,11},{11... | collective-permute-start | bytes 1304 | tf_op jit(solution)/shard_map/ppermute | solution.py:22
  196.2 5.7 %collective-permute-start.23 = (f32[3,6,6,1]{3,2,1,0:T(8,128)S(1)}, f32[3,6,6,1]{3,2,1,0:T(8,128)S(1)}, u32[]{:S(2)}, u32[]{:S(2)}) collective-permute-start(f32[3,6,6,1]{3,2,1,0:T(8,128)S(1)} %get-tuple-element.97), channel_id=1, source_target_pairs={{1,0},{2,1},{3,2},{4,3},{5,4},{6,5},{7,6},{9,8},{10,9},{11,10},{12... | collective-permute-start | bytes 1304 | tf_op jit(solution)/shard_map/ppermute | solution.py:25
  (25 other events, 38.8 us)
